TPU v7x, 256 devices: a whole 4x4x8 slice. The times are simulated.
256 devices in a mesh: pair: 32 (over z, x_lo, core), grp: 8 (over y, x_hi).
Axes of the slice: x: 4 (x_hi: 2, x_lo: 2; x = x_hi * 2 + x_lo), y: 4, z: 8, core: 2. Of those that a mesh axis runs over, the one named last changes fastest.
Arguments:
- amplitudes: float32 [8, 224, 2048], P('grp', 'pair'), may hold values from -6 to 6
- integrals: float32 [2048, 65536], P('grp', 'pair'), may hold values from -0.375 to 0.375
- owner_blocks: int32 [16], replicated, may hold values from 0 to 15, each once
- occ_pairs: int32 [8, 2, 224], P('grp'), may hold values from 0 to 63, as said below
- vir_pairs: int32 [2, 65536], replicated, may hold values from 0 to 511, as said below
- occ_energy: float32 [64], replicated, may hold values from -1.5 to -0.5
- vir_energy: float32 [512], replicated, may hold values from 0.2 to 1.5
Outputs:
- ladder: float32 [8, 224, 65536], P('grp', 'pair')
Inputs may be any that keep to these rules, and one draw needn't show every extreme that they name: `occ_pairs`: each column is a pair i<j; no pair occurs twice. `vir_pairs`: each column is a pair a<b; no pair occurs twice. `owner_blocks`: a permutation.
All inputs are finite; a program needn't handle non-finite values.
Results may differ from a plain program's by a relative error of at most 0.000071.
Values sent between devices are 32-bit elements; how exact they have to be, the bound alone decides.
No kernel may reach another device: no remote copies, remote signals or barrier semaphores. Data moves between devices by JAX's collectives and lax.ppermute only.
A program may use at most 64 MiB of HBM per device.

v0:
```python
import jax
import jax.numpy as jnp
from jax import lax
from jax.sharding import PartitionSpec as P


def pair_energies(energy, pairs):
    return jnp.take(energy, pairs[0]) + jnp.take(energy, pairs[1])


def on_device(amplitudes, integrals, owner_blocks, occ_pairs, vir_pairs, occ_energy, vir_energy):
    block = integrals.shape[0]
    columns = integrals.shape[1]
    groups = lax.axis_size("grp")
    nblocks = owner_blocks.shape[0]
    sub_width = block * groups // nblocks
    group_rows = lax.all_gather(amplitudes, "pair", axis=1, tiled=True)[0]
    piece = lax.all_gather(integrals, "grp", axis=0, tiled=True)
    count = piece.shape[0]
    rows = jnp.arange(count, dtype=jnp.int32)
    owner = jnp.take(owner_blocks, rows // sub_width)
    picked = owner * sub_width + rows % sub_width
    chosen = jnp.take(group_rows, picked, axis=1)
    work = jnp.dot(
        chosen, piece, precision=lax.Precision.HIGHEST, preferred_element_type=jnp.float32
    )
    occ_sum = pair_energies(occ_energy, occ_pairs[0])
    vir_local = lax.dynamic_slice_in_dim(vir_pairs, lax.axis_index("pair") * columns, columns, 1)
    vir_sum = pair_energies(vir_energy, vir_local)
    payload = work / (occ_sum[:, None] - vir_sum[None, :])
    return lax.all_to_all(payload[None], "pair", split_axis=1, concat_axis=2, tiled=True)


def solution(mesh):
    return jax.shard_map(
        on_device,
        mesh=mesh,
        in_specs=(
            P("grp", "pair", None),
            P("grp", "pair"),
            P(),
            P("grp", None, None),
            P(),
            P(),
            P(),
        ),
        out_specs=P("grp", "pair", None),
        check_vma=False,
    )
```

profile of v0, /device:TPU:1, one launch (start us, length us, event | category | flops | bytes accessed | tf_op | source)
XLA Modules:
  0.0 351.4 jit_solution(17929817763536348124)
XLA Ops:
  6.5 0.0 copy-start
  6.5 0.0 all-gather.3.cloned.1.call-start
  6.5 0.7 all-gather.3.cloned.1.call-update
  7.3 0.0 all-gather.5.cloned.1.call-start
  7.3 0.7 all-gather.5.cloned.1.call-update
  8.0 0.9 constant_dynamic-slice_fusion
  8.9 0.0 copy-done
  8.9 13.2 %gather_fusion.3 = f32[2048]{0:T(1024)S(1)} fusion(f32[512]{0:T(512)S(1)} %copy-done, s32[2048]{0:T(1024)S(1)} %fusion.16), kind=kCustom, calls=%fused_computation.1.clone | custom fusion | bytes 24576 | tf_op jit(solution)/shard_map/jit(_take)/gather | solution.py:8
  22.1 0.0 copy-start.3
  22.1 0.0 copy-start.1
  22.1 13.2 %gather_fusion.4 = f32[2048]{0:T(1024)S(1)} fusion(f32[512]{0:T(512)S(1)} %copy-done, s32[2048]{0:T(1024)S(1)} %fusion.17), kind=kCustom, calls=%fused_computation.3.clone | custom fusion | bytes 24576 | tf_op jit(solution)/shard_map/jit(_take)/gather | solution.py:8
  35.3 0.0 copy-done.3
  35.4 0.0 copy-start.2
  35.4 0.0 copy-done.1
  35.4 1.9 gather_fusion.1
  37.3 1.9 gather_fusion.2
  39.6 0.0 copy-done.2
  39.6 0.7 fusion.21
  40.3 4.4 %compare_select_fusion.2 = s32[2048,1]{0,1:T(1,128)S(1)} fusion(s32[]{:T(128)} %bitcast.9, s32[]{:T(128)} %bitcast.10, s32[]{:T(128)} %bitcast.11, s32[]{:T(128)} %bitcast.12, s32[]{:T(128)} %bitcast.13, s32[]{:T(128)} %bitcast.15, s32[]{:T(128)} %bitcast.14), kind=kLoop, calls=%fused_computation.21 | loop fusion | flops 47104 | bytes 8220 | tf_op jit(solution)/shard_map/jit(_take)/gather | solution.py:21
  44.8 5.7 %compare_and_fusion = (pred[2048]{0:T(1024)(128)(4,1)S(1)}, s32[2048]{0:T(1024)S(1)}) fusion(pred[2048]{0:T(1024)(128)(4,1)S(1)} %compare_reduce_fusion, pred[2048]{0:T(1024)(128)(4,1)S(1)} %compare_reduce_fusion.1, pred[2048]{0:T(1024)(128)(4,1)S(1)} %compare_reduce_fusion.2, pred[2048]{0:T(1024)(128)(4,1)S(1)} %compare_reduce_fusion.3, ...), kind=kLoop, calls=%fused_computation.55 | loop fusion | flops 73728 | bytes 36900 | tf_op jit(solution)/shard_map/jit(_take)/and | solution.py:23
  50.5 27.1 %all-gather.3.cloned.1.call-done = f32[1,224,2048]{2,0,1:T(1,128)} async-done(((f32[1,7,2048]{2,0,1:T(1,128)}), f32[1,224,2048]{2,0,1:T(1,128)}) %all-gather.3.cloned.1.call-update) | async-done | bytes 1835024 | tf_op jit(solution)/shard_map/all_gather | solution.py:17
  77.6 4.1 %copy.13 = f32[1,224,2048]{1,2,0:T(8,128)S(1)} copy(f32[1,224,2048]{2,0,1:T(1,128)} %all-gather.3.cloned.1.call-done) | data formatting | bytes 3670016 | tf_op jit(solution)/shard_map/all_gather | solution.py:17
  81.6 8.6 %gather_fusion = f32[2048,224]{1,0:T(8,128)} fusion(f32[224,2048]{0,1:T(8,128)S(1)} %bitcast.32, s32[2048]{0:T(1024)S(1)} %broadcast_clamp_fusion), kind=kCustom, calls=%fused_computation.4 | custom fusion | bytes 3678208 | tf_op jit(solution)/shard_map/jit(_take)/gather | solution.py:23
  90.2 175.9 %all-gather.5.cloned.1.call-done = f32[2048,2048]{1,0:T(8,128)} async-done(((f32[256,2048]{1,0:T(8,128)}), f32[2048,2048]{1,0:T(8,128)}) %all-gather.5.cloned.1.call-update) | async-done | bytes 16777232 | tf_op jit(solution)/shard_map/all_gather | solution.py:18
  266.1 20.5 %fusion = f32[1,224,2048]{2,1,0:T(8,128)S(1)} fusion(f32[2048,2048]{1,0:T(8,128)} %all-gather.5.cloned.1.call-done, f32[2048,224]{1,0:T(8,128)} %gather_fusion, pred[2048]{0:T(1024)(128)(4,1)S(1)} %get-tuple-element.6, f32[2048]{0:T(1024)S(1)} %select_add_fusion, f32[224]{0:T(256)S(1)} %fusion.18), kind=kOutput, calls=%fused_computation.6 | convolution fusion | flops 11275665408 | bytes 20458368 | tf_op jit(solution)/shard_map/dot_general | solution.py:24
  286.6 1.9 copy.14
  288.5 53.5 %all_to_all.18 = f32[1,224,2048]{2,0,1:T(1,128)S(1)} all-to-all(f32[1,224,2048]{2,0,1:T(1,128)S(1)} %copy.14), channel_id=1, replica_groups=mesh['pair'=32,'grp'=8] {'pair'}, dimensions={1} | all-to-all | bytes 3670016 | tf_op jit(solution)/shard_map/all_to_all | solution.py:31
  342.0 2.6 copy.16
  (20 shorter events, 0.5 us)
Async XLA Ops:
  6.5 2.4 copy-start
  6.5 71.0 %all-gather.3.cloned.1.call-start = ((), (), s32[]{:S(2)}) async-start(), calls=%async_computation.1 | async-start | bytes 1892352 | tf_op jit(solution)/shard_map/all_gather | solution.py:17
  7.3 258.8 %all-gather.5.cloned.1.call-start = ((), (), s32[]{:S(2)}) async-start(), calls=%async_computation.2 | async-start | bytes 18874368 | tf_op jit(solution)/shard_map/all_gather | solution.py:18
  22.1 13.2 %copy-start.3 = (s32[1,2,224]{2,1,0:T(2,128)S(1)}, s32[1,2,224]{2,1,0:T(2,128)}, u32[]{:S(2)}) copy-start(s32[1,2,224]{2,1,0:T(2,128)} %param.14) | copy-start | bytes 5380
  22.1 13.3 %copy-start.1 = (f32[64]{0:T(128)S(1)}, f32[64]{0:T(128)}, u32[]{:S(2)}) copy-start(f32[64]{0:T(128)} %param.16) | copy-start | bytes 772
  35.4 4.2 %copy-start.2 = (s32[16]{0:T(128)S(1)}, s32[16]{0:T(128)}, u32[]{:S(2)}) copy-start(s32[16]{0:T(128)} %param.13) | copy-start | bytes 196
Sparse Core Ops, SparseCore 0:
  9.2 68.3 all-gather.2
  80.2 185.8 all-gather.4
where the time goes:
time: 352 us; the launch traced here: 351 us
  waiting for transfers between devices  204 us (58%)
  blocking collectives  53.5 us (15%)
  local copies, waits for them, and re-layouts  48.8 us (14%)
  matrix products  20.5 us (6%)
  between operations  13.6 us (4%)
  other arithmetic  10.5 us (3%)
    all_gather x1, waiting for transfers between devices, on_device(): piece = lax.all_gather(integrals, 'grp', axis=0, tiled=True)  176 us
    all_to_all x1, blocking collectives, on_device(): lax.all_to_all(payload[None], 'pair', split_axis=1, concat_axis=2, tiled=...  53.5 us
    gather x4, local copies, waits for them, and re-layouts, pair_energies(): return jnp.take(energy, pairs[0]) + jnp.take(energy, pairs[1])  30.1 us
    all_gather x1, waiting for transfers between devices, on_device(): group_rows = lax.all_gather(amplitudes, 'pair', axis=1, tiled=True)[0]  27.1 us
    dot_general x1, matrix products, on_device(): jnp.dot(chosen, piece, precision=lax.Precision.HIGHEST, preferred_element...  20.5 us
    gather x1, local copies, waits for them, and re-layouts, on_device(): chosen = jnp.take(group_rows, picked, axis=1)  8.56 us
  transfers between devices with their start and end apart: 2, of which 2 were waited for; matrix products, arithmetic and copies ran while one was open for 16% of the time, Pallas kernels for 0%

commit v1 on v0

--- a/solution.py
+++ b/solution.py
@@ -15,7 +15,15 @@
     nblocks = owner_blocks.shape[0]
     sub_width = block * groups // nblocks
     group_rows = lax.all_gather(amplitudes, "pair", axis=1, tiled=True)[0]
-    piece = lax.all_gather(integrals, "grp", axis=0, tiled=True)
+
+    def edit_chunk_over_axis(vals, mesh_dim="grp"):
+        reply = jax.lax.psum(1, axis_name=mesh_dim)
+        k_now = jax.lax.all_to_all(
+            jnp.stack(reply * [vals], axis=0), axis_name=mesh_dim, split_axis=0, concat_axis=0
+        )
+        return jnp.concatenate(k_now, 0)
+
+    piece = edit_chunk_over_axis(integrals)
     count = piece.shape[0]
     rows = jnp.arange(count, dtype=jnp.int32)
     owner = jnp.take(owner_blocks, rows // sub_width)

time: 352 us -> 304 us (0.86)
  waiting for transfers between devices: 204 us -> 138 us
  local copies, waits for them, and re-layouts: 48.8 us -> 58.3 us
  starting transfers between devices: 0.04 us -> 7.51 us
    all_gather x1 -> x0, waiting for transfers between devices: 176 us -> none  [on_device(): piece = lax.all_gather(integrals, 'grp', axis=0, tiled=True)]
    all_to_all x0 -> x1, waiting for transfers between devices: none -> 110 us  [edit_chunk_over_axis(): jax.lax.all_to_all(jnp.stack(reply * [vals], axis=0), axis_name=mesh_dim,...]
    another operation x0 -> x1, local copies, waits for them, and re-layouts: none -> 9.45 us  [edit_chunk_over_axis(): jnp.stack(reply * [vals], axis=0)]
    all_to_all x0 -> x1, starting transfers between devices: none -> 7.47 us  [edit_chunk_over_axis(): jax.lax.all_to_all(jnp.stack(reply * [vals], axis=0), axis_name=mesh_dim,...]
  transfers between devices with their start and end apart: 2 -> 2, of which waited for: 2 -> 2; matrix products, arithmetic and copies ran while one was open for 16% -> 18% of each run, Pallas kernels for 0% -> 0%
where the time goes in v1:
time: 304 us
  waiting for transfers between devices  138 us (45%)
  local copies, waits for them, and re-layouts  58.3 us (19%)
  blocking collectives  54.5 us (18%)
  matrix products  20.5 us (7%)
  between operations  13.6 us (4%)
  other arithmetic  10.8 us (4%)
  starting transfers between devices  7.51 us (2%)
    all_to_all x1, waiting for transfers between devices, edit_chunk_over_axis(): jax.lax.all_to_all(jnp.stack(reply * [vals], axis=0), axis_name=mesh_dim,...  110 us
    all_to_all x1, blocking collectives, on_device(): lax.all_to_all(payload[None], 'pair', split_axis=1, concat_axis=2, tiled=...  54.5 us
    gather x4, local copies, waits for them, and re-layouts, pair_energies(): return jnp.take(energy, pairs[0]) + jnp.take(energy, pairs[1])  30.1 us
    all_gather x1, waiting for transfers between devices, on_device(): group_rows = lax.all_gather(amplitudes, 'pair', axis=1, tiled=True)[0]  27.4 us
    dot_general x1, matrix products, on_device(): jnp.dot(chosen, piece, precision=lax.Precision.HIGHEST, preferred_element...  20.5 us
    another operation x1, local copies, waits for them, and re-layouts, edit_chunk_over_axis(): jnp.stack(reply * [vals], axis=0)  9.45 us
    gather x1, local copies, waits for them, and re-layouts, on_device(): chosen = jnp.take(group_rows, picked, axis=1)  8.55 us
    all_to_all x1, starting transfers between devices, edit_chunk_over_axis(): jax.lax.all_to_all(jnp.stack(reply * [vals], axis=0), axis_name=mesh_dim,...  7.47 us
  transfers between devices with their start and end apart: 2, of which 2 were waited for; matrix products, arithmetic and copies ran while one was open for 18% of the time, Pallas kernels for 0%

profile of v1, /device:TPU:1, one launch (start us, length us, event | category | flops | bytes accessed | tf_op | source)
XLA Modules:
  0.0 303.5 jit_solution(1069842612828746574)
XLA Ops:
  6.5 0.0 copy-start
  6.5 9.4 %stack.2 = f32[8,256,2048]{2,1,0:T(8,128)} broadcast(f32[256,2048]{1,0:T(8,128)} %param.12), dimensions={1,2} | broadcast | bytes 18874368 | tf_op jit(solution)/shard_map/stack | solution.py:22
  16.0 7.5 %all-to-all-start = ((f32[8,256,2048]{2,1,0:T(8,128)}), f32[8,256,2048]{2,1,0:T(8,128)}, u32[]{:S(2)}, u32[]{:S(2)}) async-start(f32[8,256,2048]{2,1,0:T(8,128)} %stack.2), calls=%async_computation | async-start | bytes 33554432 | tf_op jit(solution)/shard_map/all_to_all | solution.py:21
  23.5 0.0 all-gather.2.cloned.1.call-start
  23.5 0.7 all-gather.2.cloned.1.call-update
  24.2 0.9 constant_dynamic-slice_fusion
  25.1 0.0 copy-done
  25.1 13.2 %gather_fusion.4 = f32[2048]{0:T(1024)S(1)} fusion(f32[512]{0:T(512)S(1)} %copy-done, s32[2048]{0:T(1024)S(1)} %fusion.17), kind=kCustom, calls=%fused_computation.3.clone | custom fusion | bytes 24576 | tf_op jit(solution)/shard_map/jit(_take)/gather | solution.py:8
  38.3 0.0 copy-start.3
  38.3 0.0 copy-start.1
  38.3 13.2 %gather_fusion.3 = f32[2048]{0:T(1024)S(1)} fusion(f32[512]{0:T(512)S(1)} %copy-done, s32[2048]{0:T(1024)S(1)} %fusion.16), kind=kCustom, calls=%fused_computation.1.clone | custom fusion | bytes 24576 | tf_op jit(solution)/shard_map/jit(_take)/gather | solution.py:8
  51.5 0.0 copy-done.3
  51.5 0.0 copy-start.2
  51.6 0.0 copy-done.1
  51.6 1.9 gather_fusion.1
  53.5 1.9 gather_fusion.2
  55.8 0.0 copy-done.2
  55.8 0.7 fusion.21
  56.5 4.5 %compare_select_fusion.2 = s32[2048,1]{0,1:T(1,128)S(1)} fusion(s32[]{:T(128)} %bitcast.9, s32[]{:T(128)} %bitcast.10, s32[]{:T(128)} %bitcast.11, s32[]{:T(128)} %bitcast.12, s32[]{:T(128)} %bitcast.13, s32[]{:T(128)} %bitcast.15, s32[]{:T(128)} %bitcast.14), kind=kLoop, calls=%fused_computation.21 | loop fusion | flops 47104 | bytes 8220 | tf_op jit(solution)/shard_map/jit(_take)/gather | solution.py:29
  61.0 5.9 %compare_and_fusion = (pred[2048]{0:T(1024)(128)(4,1)S(1)}, s32[2048]{0:T(1024)S(1)}) fusion(pred[2048]{0:T(1024)(128)(4,1)S(1)} %compare_reduce_fusion, pred[2048]{0:T(1024)(128)(4,1)S(1)} %compare_reduce_fusion.1, pred[2048]{0:T(1024)(128)(4,1)S(1)} %compare_reduce_fusion.2, pred[2048]{0:T(1024)(128)(4,1)S(1)} %compare_reduce_fusion.3, ...), kind=kLoop, calls=%fused_computation.55 | loop fusion | flops 73728 | bytes 36900 | tf_op jit(solution)/shard_map/jit(_take)/and | solution.py:31
  66.9 27.4 %all-gather.2.cloned.1.call-done = f32[1,224,2048]{2,0,1:T(1,128)} async-done(((f32[1,7,2048]{2,0,1:T(1,128)}), f32[1,224,2048]{2,0,1:T(1,128)}) %all-gather.2.cloned.1.call-update) | async-done | bytes 1835024 | tf_op jit(solution)/shard_map/all_gather | solution.py:17
  94.3 4.1 %copy.13 = f32[1,224,2048]{1,2,0:T(8,128)S(1)} copy(f32[1,224,2048]{2,0,1:T(1,128)} %all-gather.2.cloned.1.call-done) | data formatting | bytes 3670016 | tf_op jit(solution)/shard_map/all_gather | solution.py:17
  98.3 8.5 %gather_fusion = f32[2048,224]{1,0:T(8,128)} fusion(f32[224,2048]{0,1:T(8,128)S(1)} %bitcast.33, s32[2048]{0:T(1024)S(1)} %broadcast_clamp_fusion), kind=kCustom, calls=%fused_computation.4 | custom fusion | bytes 3678208 | tf_op jit(solution)/shard_map/jit(_take)/gather | solution.py:31
  106.9 110.3 %all-to-all-done = f32[8,256,2048]{2,1,0:T(8,128)} async-done(((f32[8,256,2048]{2,1,0:T(8,128)}), f32[8,256,2048]{2,1,0:T(8,128)}, u32[]{:S(2)}, u32[]{:S(2)}) %all-to-all-start) | async-done | bytes 16777248 | tf_op jit(solution)/shard_map/all_to_all | solution.py:21
  217.2 20.5 %fusion = f32[1,224,2048]{2,1,0:T(8,128)S(1)} fusion(f32[2048,2048]{1,0:T(8,128)} %bitcast.20, f32[2048,224]{1,0:T(8,128)} %gather_fusion, pred[2048]{0:T(1024)(128)(4,1)S(1)} %get-tuple-element.6, f32[2048]{0:T(1024)S(1)} %select_add_fusion, f32[224]{0:T(256)S(1)} %fusion.18), kind=kOutput, calls=%fused_computation.6 | convolution fusion | flops 11275665408 | bytes 20458368 | tf_op jit(solution)/shard_map/dot_general | solution.py:32
  237.7 1.9 copy.14
  239.6 54.5 %all_to_all.23 = f32[1,224,2048]{2,0,1:T(1,128)S(1)} all-to-all(f32[1,224,2048]{2,0,1:T(1,128)S(1)} %copy.14), channel_id=1, replica_groups=mesh['pair'=32,'grp'=8] {'pair'}, dimensions={1} | all-to-all | bytes 3670016 | tf_op jit(solution)/shard_map/all_to_all | solution.py:39
  294.1 2.6 copy.16
  (20 shorter events, 0.5 us)
Async XLA Ops:
  6.5 18.6 %copy-start = (f32[512]{0:T(512)S(1)}, f32[512]{0:T(512)}, u32[]{:S(2)}) copy-start(f32[512]{0:T(512)} %param.17) | copy-start | bytes 6148
  16.0 201.2 %all-to-all-start = ((f32[8,256,2048]{2,1,0:T(8,128)}), f32[8,256,2048]{2,1,0:T(8,128)}, u32[]{:S(2)}, u32[]{:S(2)}) async-start(f32[8,256,2048]{2,1,0:T(8,128)} %stack.2), calls=%async_computation | async-start | bytes 33554432 | tf_op jit(solution)/shard_map/all_to_all | solution.py:21
  23.5 70.8 %all-gather.2.cloned.1.call-start = ((), (), s32[]{:S(2)}) async-start(), calls=%async_computation.2 | async-start | bytes 1892352 | tf_op jit(solution)/shard_map/all_gather | solution.py:17
  38.3 13.2 %copy-start.3 = (s32[1,2,224]{2,1,0:T(2,128)S(1)}, s32[1,2,224]{2,1,0:T(2,128)}, u32[]{:S(2)}) copy-start(s32[1,2,224]{2,1,0:T(2,128)} %param.14) | copy-start | bytes 5380
  38.3 13.3 %copy-start.1 = (f32[64]{0:T(128)S(1)}, f32[64]{0:T(128)}, u32[]{:S(2)}) copy-start(f32[64]{0:T(128)} %param.16) | copy-start | bytes 772
  51.5 4.2 %copy-start.2 = (s32[16]{0:T(128)S(1)}, s32[16]{0:T(128)}, u32[]{:S(2)}) copy-start(s32[16]{0:T(128)} %param.13) | copy-start | bytes 196
Sparse Core Ops, SparseCore 0:
  26.1 68.1 all-gather.1
